TPU v7x, 256 devices: a whole 4x4x8 slice. The times are simulated.
256 devices in a mesh: det: 16 (over z, core), orb: 16 (over x, y).
Axes of the slice: x: 4, y: 4, z: 8, core: 2. Of those that a mesh axis runs over, the one named last changes fastest.
Arguments:
- orbitals: bfloat16 [64, 1024, 256], P('det', 'orb'), may hold values from -0.06 to 1.06
- dfit: bfloat16 [64, 1024, 1024], P('orb'), may hold values from -0.5 to 0.5, as said below
- pair_left: int32 [32], P('det'), may hold values from 0 to 63, as said below
- pair_right: int32 [32], P('det'), may hold values from 0 to 63
- pair_count: int32 [16], P('det'), may hold values from 1 to 2, as said below
- pair_weight: float32 [32], P('det'), may hold values from 1 to 4
- aux_screen: int32 [32, 64], P('det', 'orb'), may hold values 0 or 1
Outputs:
- gradient: float32 [64, 1024, 256], P('det', 'orb')
Inputs may be any that keep to these rules, and one draw needn't show every extreme that they name: `pair_left`: slot s names a determinant among numbers (s // 2) * 4 to (s // 2 + 1) * 4 - 1. `pair_count`: some det index has all 2 slots live. `dfit`: every matrix is symmetric.
All inputs are finite; a program needn't handle non-finite values. No bound on the sum of `aux_screen` on one device may be relied on, other than what follows from the above.
Results may differ from a plain program's by a relative error of at most 0.0022.
Values may be sent and summed in bfloat16 or wider, within the bound.
No kernel may reach another device: no remote copies, remote signals or barrier semaphores. Data moves between devices by JAX's collectives and lax.ppermute only.
A program may use at most 64 MiB of HBM per device.

v0:
```python
import jax
import jax.numpy as jnp
from jax import lax
from jax.sharding import PartitionSpec as P

NS = 3


def newton(correlation):
    eye = jnp.eye(correlation.shape[-1], dtype=jnp.float32)
    inverse = jnp.broadcast_to(eye, correlation.shape)
    for sweep in range(NS):
        product = jnp.einsum("bij,bjk->bik", correlation, inverse, precision=lax.Precision.HIGHEST)
        inverse = jnp.einsum(
            "bij,bjk->bik", inverse, 2.0 * eye - product, precision=lax.Precision.HIGHEST
        )
    return inverse


def process(dfit, left_rows, right_rows, weights, screen):
    correlation_part = jnp.einsum(
        "brc,brd->bcd", left_rows, right_rows, preferred_element_type=jnp.float32
    )
    correlation = lax.psum(correlation_part, "orb")
    inverse = newton(correlation)
    moved_rows = jnp.einsum(
        "brc,bcd->brd", right_rows.astype(jnp.float32), inverse, precision=lax.Precision.HIGHEST
    ).astype(jnp.bfloat16)
    left_full, moved_full = (
        lax.all_gather(left_rows, "orb", axis=1, tiled=True),
        lax.all_gather(moved_rows, "orb", axis=1, tiled=True),
    )
    applied = jnp.einsum(
        "qst,btc->bqsc", dfit, moved_full, preferred_element_type=jnp.float32
    ).astype(jnp.bfloat16)
    projected = jnp.einsum(
        "bsc,qst->bqct", left_full, dfit, preferred_element_type=jnp.float32
    ).astype(jnp.bfloat16)
    exchange = jnp.einsum(
        "bqct,btd->bqcd", projected, moved_full, preferred_element_type=jnp.float32
    )
    factor = 2.0 * weights[:, None, None, None] * screen.astype(jnp.float32)[:, :, None, None]
    scaled = (factor * exchange).astype(jnp.bfloat16)
    left_term = jnp.einsum("bqsc,bqdc->sbd", applied, scaled, preferred_element_type=jnp.float32)
    moved_term = jnp.einsum("bqcs,bqcd->sbd", projected, scaled, preferred_element_type=jnp.float32)
    summed = lax.psum_scatter(
        jnp.concatenate([left_term, moved_term], axis=1), "orb", scatter_dimension=0, tiled=True
    )
    batch = left_rows.shape[0]
    left_grad = jnp.transpose(summed[:, :batch], (1, 0, 2))
    moved_grad = jnp.transpose(summed[:, batch:], (1, 0, 2))
    right_grad = jnp.einsum("brc,bdc->brd", moved_grad, inverse, precision=lax.Precision.HIGHEST)
    return (left_grad, right_grad)


def local(orbitals, dfit, pair_left, pair_right, pair_count, pair_weight, aux_screen):
    det_local = orbitals.shape[0]
    capacity = pair_left.shape[0]
    slot_index = jnp.arange(capacity, dtype=jnp.int32)
    weights = jnp.where(slot_index < pair_count[0], pair_weight, jnp.zeros_like(pair_weight))
    left_local = pair_left % det_local
    left_rows = jnp.take(orbitals, left_local, axis=0)
    everyone = lax.all_gather(orbitals, "det", axis=0, tiled=True)
    right_rows = jnp.take(everyone, pair_right, axis=0)

    def one_slot(slot, grads):

        def select_slot(array):
            return lax.dynamic_slice_in_dim(array, slot, 1, 0)

        left_one, right_one = process(
            dfit,
            select_slot(left_rows),
            select_slot(right_rows),
            select_slot(weights),
            select_slot(aux_screen),
        )
        return (
            lax.dynamic_update_slice_in_dim(grads[0], left_one, slot, 0),
            lax.dynamic_update_slice_in_dim(grads[1], right_one, slot, 0),
        )

    zeros = jnp.zeros(left_rows.shape, jnp.float32)
    left_grad, right_grad = lax.fori_loop(0, capacity, one_slot, (zeros, zeros))
    owners = (left_local[:, None] == jnp.arange(det_local, dtype=jnp.int32)[None, :]).astype(
        jnp.float32
    )
    own_sum = jnp.einsum("pn,prc->nrc", owners, left_grad, precision=lax.Precision.HIGHEST)
    places = jnp.arange(det_local * lax.axis_size("det"), dtype=jnp.int32)
    match = (pair_right[:, None] == places[None, :]).astype(jnp.float32)
    returned = lax.psum_scatter(
        jnp.einsum("pn,prc->nrc", match, right_grad, precision=lax.Precision.HIGHEST),
        "det",
        scatter_dimension=0,
        tiled=True,
    )
    return own_sum + returned


def solution(mesh):
    in_specs = (
        P("det", "orb", None),
        P("orb", None, None),
        P("det"),
        P("det"),
        P("det"),
        P("det"),
        P("det", "orb"),
    )
    out_specs = P("det", "orb", None)
    return jax.shard_map(local, mesh=mesh, in_specs=in_specs, out_specs=out_specs, check_vma=False)
```

profile of v0, /device:TPU:4, one launch (start us, length us, event | category | flops | bytes accessed | tf_op | source)
XLA Modules:
  0.0 620.7 jit_solution(5396601231880543745)
XLA Ops:
  8.6 1.5 gather_fusion
  12.1 39.4 %all-gather.5.cloned.1.call-done = bf16[64,64,256]{2,1,0:T(8,128)(2,1)} async-done(((bf16[4,64,256]{2,1,0:T(8,128)(2,1)}), bf16[64,64,256]{2,1,0:T(8,128)(2,1)}) %all-gather.5.cloned.1.call-update) | async-done | bytes 2097168 | tf_op jit(solution)/shard_map/all_gather | solution.py:63
  51.6 2.1 gather_fusion.1
  53.8 486.6 %while.15 = (s32[]{:T(128)}, f32[2,64,256]{2,0,1:T(2,128)}, f32[2,64,256]{2,0,1:T(2,128)}, f32[2]{0:T(128)S(1)}, s32[2,4]{1,0:T(2,128)}, /*index=5*/bf16[2,64,25...) while((s32[]{:T(128)}, f32[2,64,256]{2,0,1:T(2,128)}, ...), condition=%wide.region_3.4_spmd, body=%wide.region_0.3_spmd.sunk | while | flops 7227064320 | bytes 65279744 | solution.py:84
  53.9 0.9 fusion.130
  54.9 23.7 %all_gather.19 = bf16[1,1024,256]{2,1,0:T(8,128)(2,1)S(1)} all-gather(bf16[1,64,256]{2,1,0:T(8,128)(2,1)S(1)} %constant_dynamic-slice_fusion.6), channel_id=1, replica_groups=mesh['det'=16,'orb'=16] {'orb'}, dimensions={1}, use_global_device_ids=true | all-gather | bytes 557056 | tf_op jit(solution)/shard_map/while/body/eval_jaxpr/all_gather | solution.py:30
  78.5 5.8 convolution_convert_fusion.4
  85.6 64.8 %all-reduce.6.cloned.1.call-done = f32[256,256]{1,0:T(8,128)} async-done(((f32[256,256]{1,0:T(8,128)}), f32[256,256]{1,0:T(8,128)}) %all-reduce.6.cloned.1.call-update) | async-done | bytes 262160 | tf_op jit(solution)/shard_map/while/body/eval_jaxpr/psum | solution.py:24
  150.4 1.3 convolution_subtract_fusion.6
  152.0 1.3 convolution_subtract_fusion.7
  154.7 22.7 %all-gather.2 = bf16[1024,256]{1,0:T(8,128)(2,1)S(1)} all-gather(bf16[64,256]{1,0:T(8,128)(2,1)S(1)} %convolution_convert_fusion.5), channel_id=2, replica_groups=mesh['det'=16,'orb'=16] {'orb'}, dimensions={0}, use_global_device_ids=true | all-gather | bytes 557056 | tf_op jit(solution)/shard_map/while/body/eval_jaxpr/all_gather | solution.py:31
  180.5 7.7 %fusion.137 = f32[1024,1,256]{0,2,1:T(8,128)} fusion(bf16[4,256,256]{2,1,0:T(8,128)(2,1)} %copy-done.1, bf16[4,1024,1024]{2,1,0:T(8,128)(2,1)} %get-tuple-element.280, bf16[1024,256]{1,0:T(8,128)(2,1)} %copy-done.2), kind=kOutput, calls=%fused_computation.12.clone.1 | convolution fusion | flops 2685403136 | bytes 10485760 | tf_op jit(solution)/shard_map/while/body/eval_jaxpr/bqsc,bqdc->sbd/dot_general | solution.py:44
  188.2 1.4 pad_maximum_fusion.2
  189.6 2.4 copy.46
  193.8 98.1 %all-reduce.8.cloned.1.call-done = f32[1024,2,256]{2,1,0:T(2,128)} async-done(((f32[1024,2,256]{2,1,0:T(2,128)}), f32[1024,2,256]{2,1,0:T(2,128)}) %all-reduce.8.cloned.1.call-update) | async-done | bytes 2097168 | tf_op jit(solution)/shard_map/while
  291.9 1.1 constant_dynamic-slice_fusion.7
  293.5 0.9 dynamic_update_slice.16
  297.0 23.4 %all_gather.19 = bf16[1,1024,256]{2,1,0:T(8,128)(2,1)S(1)} all-gather(bf16[1,64,256]{2,1,0:T(8,128)(2,1)S(1)} %constant_dynamic-slice_fusion.6), channel_id=1, replica_groups=mesh['det'=16,'orb'=16] {'orb'}, dimensions={1}, use_global_device_ids=true | all-gather | bytes 557056 | tf_op jit(solution)/shard_map/while/body/eval_jaxpr/all_gather | solution.py:30
  320.4 5.8 convolution_convert_fusion.4
  327.4 67.3 %all-reduce.6.cloned.1.call-done = f32[256,256]{1,0:T(8,128)} async-done(((f32[256,256]{1,0:T(8,128)}), f32[256,256]{1,0:T(8,128)}) %all-reduce.6.cloned.1.call-update) | async-done | bytes 262160 | tf_op jit(solution)/shard_map/while/body/eval_jaxpr/psum | solution.py:24
  394.7 1.3 convolution_subtract_fusion.6
  396.3 1.3 convolution_subtract_fusion.7
  399.1 22.7 %all-gather.2 = bf16[1024,256]{1,0:T(8,128)(2,1)S(1)} all-gather(bf16[64,256]{1,0:T(8,128)(2,1)S(1)} %convolution_convert_fusion.5), channel_id=2, replica_groups=mesh['det'=16,'orb'=16] {'orb'}, dimensions={0}, use_global_device_ids=true | all-gather | bytes 557056 | tf_op jit(solution)/shard_map/while/body/eval_jaxpr/all_gather | solution.py:31
  424.9 7.7 %fusion.137 = f32[1024,1,256]{0,2,1:T(8,128)} fusion(bf16[4,256,256]{2,1,0:T(8,128)(2,1)} %copy-done.1, bf16[4,1024,1024]{2,1,0:T(8,128)(2,1)} %get-tuple-element.280, bf16[1024,256]{1,0:T(8,128)(2,1)} %copy-done.2), kind=kOutput, calls=%fused_computation.12.clone.1 | convolution fusion | flops 2685403136 | bytes 10485760 | tf_op jit(solution)/shard_map/while/body/eval_jaxpr/bqsc,bqdc->sbd/dot_general | solution.py:44
  432.5 1.4 pad_maximum_fusion.2
  433.9 2.4 copy.46
  438.2 98.1 %all-reduce.8.cloned.1.call-done = f32[1024,2,256]{2,1,0:T(2,128)} async-done(((f32[1024,2,256]{2,1,0:T(2,128)}), f32[1024,2,256]{2,1,0:T(2,128)}) %all-reduce.8.cloned.1.call-update) | async-done | bytes 2097168 | tf_op jit(solution)/shard_map/while
  536.3 1.1 constant_dynamic-slice_fusion.7
  540.4 2.8 fusion.39
  543.2 4.4 copy.30
  549.0 63.2 %reduce-scatter.2.cloned.1.call-done = f32[4,64,256]{2,1,0:T(8,128)} async-done(((f32[64,64,256]{2,1,0:T(8,128)}), f32[4,64,256]{2,1,0:T(8,128)}) %reduce-scatter.2.cloned.1.call-update) | async-done | bytes 262160 | tf_op jit(solution)/shard_map/reduce_scatter | solution.py:91
  612.2 1.7 copy_add_fusion
  (94 shorter events, 24.1 us)
Async XLA Ops:
  6.5 45.0 %all-gather.5.cloned.1.call-start = ((), (), s32[]{:S(2)}) async-start(), calls=%async_computation.1 | async-start | bytes 2228224 | tf_op jit(solution)/shard_map/all_gather | solution.py:63
  53.8 486.6 %copy-start.9 = (s32[2]{0:T(128)S(1)}, s32[2]{0:T(128)}, u32[]{:S(2)}) copy-start(s32[2]{0:T(128)} %param.12) | copy-start | bytes 28
  53.8 96.5 %all-reduce.6.cloned.1.call-start = ((), (), s32[]{:S(2)}) async-start(), calls=%async_computation.3 | async-start | bytes 524288 | tf_op jit(solution)/shard_map/while/body/eval_jaxpr/psum | solution.py:24
  54.8 237.1 %all-reduce.8.cloned.1.call-start = ((), (), s32[]{:S(2)}) async-start(), calls=%async_computation.4 | async-start | bytes 4194304 | tf_op jit(solution)/shard_map/while
  78.5 7.0 %copy-start.8 = (s32[2,4]{1,0:T(2,128)S(1)}, s32[2,4]{1,0:T(2,128)}, u32[]{:S(2)}) copy-start(s32[2,4]{1,0:T(2,128)} %get-tuple-element.278) | copy-start | bytes 100 | tf_op jit(solution)/shard_map/while
  150.4 3.3 copy-start
  177.4 0.8 copy-start.2
  179.0 0.8 copy-start.1
  191.9 0.7 copy-start.10
  192.0 101.5 %copy-start.5 = (f32[2,64,256]{2,0,1:T(2,128)S(1)}, f32[2,64,256]{2,0,1:T(2,128)}, u32[]{:S(2)}) copy-start(f32[2,64,256]{2,0,1:T(2,128)} %get-tuple-element.260) | copy-start | bytes 393220 | tf_op jit(solution)/shard_map/while
  192.0 102.5 %copy-start.3 = (f32[2,64,256]{2,0,1:T(2,128)S(1)}, f32[2,64,256]{2,0,1:T(2,128)}, u32[]{:S(2)}) copy-start(f32[2,64,256]{2,0,1:T(2,128)} %get-tuple-element.261) | copy-start | bytes 393220 | tf_op jit(solution)/shard_map/while
  294.4 1.0 copy-start.6
  295.4 0.6 copy-start.4
  296.0 98.7 %all-reduce.6.cloned.1.call-start = ((), (), s32[]{:S(2)}) async-start(), calls=%async_computation.3 | async-start | bytes 524288 | tf_op jit(solution)/shard_map/while/body/eval_jaxpr/psum | solution.py:24
  296.9 239.4 %all-reduce.8.cloned.1.call-start = ((), (), s32[]{:S(2)}) async-start(), calls=%async_computation.4 | async-start | bytes 4194304 | tf_op jit(solution)/shard_map/while
  320.4 7.0 %copy-start.8 = (s32[2,4]{1,0:T(2,128)S(1)}, s32[2,4]{1,0:T(2,128)}, u32[]{:S(2)}) copy-start(s32[2,4]{1,0:T(2,128)} %get-tuple-element.278) | copy-start | bytes 100 | tf_op jit(solution)/shard_map/while
  394.7 3.3 copy-start
  421.8 0.8 copy-start.2
  423.3 0.8 copy-start.1
  436.3 0.7 copy-start.10
  436.3 101.5 %copy-start.5 = (f32[2,64,256]{2,0,1:T(2,128)S(1)}, f32[2,64,256]{2,0,1:T(2,128)}, u32[]{:S(2)}) copy-start(f32[2,64,256]{2,0,1:T(2,128)} %get-tuple-element.260) | copy-start | bytes 393220 | tf_op jit(solution)/shard_map/while
  436.3 102.5 %copy-start.3 = (f32[2,64,256]{2,0,1:T(2,128)S(1)}, f32[2,64,256]{2,0,1:T(2,128)}, u32[]{:S(2)}) copy-start(f32[2,64,256]{2,0,1:T(2,128)} %get-tuple-element.261) | copy-start | bytes 393220 | tf_op jit(solution)/shard_map/while
  538.8 1.0 copy-start.6
  539.7 0.6 copy-start.4
  540.4 71.8 %reduce-scatter.2.cloned.1.call-start = ((), (), s32[]{:S(2)}) async-start(), calls=%async_computation.2 | async-start | bytes 4456448 | tf_op jit(solution)/shard_map/reduce_scatter | solution.py:91
  547.6 0.9 copy-start.7
Sparse Core Ops, SparseCore 0:
  9.2 42.3 all-gather.4
  57.8 92.5 all-reduce.5
  192.1 99.8 all-reduce.7
  299.7 94.9 all-reduce.5
  436.4 99.8 all-reduce.7
  547.7 64.3 reduce-scatter.1
where the time goes:
time: 621 us
  waiting for transfers between devices  432 us (70%)
  blocking collectives  92.5 us (15%)
  matrix products  44.2 us (7%)
  local copies, waits for them, and re-layouts  27.8 us (4%)
  between operations  14.1 us (2%)
  other arithmetic  7.37 us (1%)
    while x6, waiting for transfers between devices  196 us
    psum x2, waiting for transfers between devices, process(): correlation = lax.psum(correlation_part, 'orb')  132 us
    reduce_scatter x1, waiting for transfers between devices, local(): lax.psum_scatter(jnp.einsum('pn,prc->nrc', match, right_grad, precision=l...  63.2 us
    all_gather x2, blocking collectives, process(): lax.all_gather(left_rows, 'orb', axis=1, tiled=True)  47 us
    all_gather x2, blocking collectives, process(): lax.all_gather(moved_rows, 'orb', axis=1, tiled=True)  45.4 us
    all_gather x1, waiting for transfers between devices, local(): everyone = lax.all_gather(orbitals, 'det', axis=0, tiled=True)  39.4 us
    dot_general x2, matrix products, process(): jnp.einsum('bqsc,bqdc->sbd', applied, scaled, preferred_element_type=jnp....  15.3 us
  transfers between devices with their start and end apart: 6, of which 6 were waited for; matrix products, arithmetic and copies ran while one was open for 3% of the time, Pallas kernels for 0%

commit v1 on v0

--- a/solution.py
+++ b/solution.py
@@ -21,7 +21,7 @@
     correlation_part = jnp.einsum(
         "brc,brd->bcd", left_rows, right_rows, preferred_element_type=jnp.float32
     )
-    correlation = lax.psum(correlation_part, "orb")
+    correlation = jnp.sum(lax.all_gather(correlation_part, "orb"), axis=0)
     inverse = newton(correlation)
     moved_rows = jnp.einsum(
         "brc,bcd->brd", right_rows.astype(jnp.float32), inverse, precision=lax.Precision.HIGHEST

time: 621 us -> 546 us (0.88)
  waiting for transfers between devices: 432 us -> 354 us
  other arithmetic: 7.37 us -> 13.7 us
    psum x2 -> x0, waiting for transfers between devices: 132 us -> none  [process(): correlation = lax.psum(correlation_part, 'orb')]
    all_gather x0 -> x2, waiting for transfers between devices: none -> 54 us  [process(): correlation = jnp.sum(lax.all_gather(correlation_part, 'orb'), axis=0)]
  transfers between devices with their start and end apart: 6 -> 6, of which waited for: 6 -> 6; matrix products, arithmetic and copies ran while one was open for 3% -> 4% of each run, Pallas kernels for 0% -> 0%
where the time goes in v1:
time: 546 us; the launch traced here: 545 us
  waiting for transfers between devices  354 us (65%)
  blocking collectives  92.4 us (17%)
  matrix products  40.2 us (7%)
  local copies, waits for them, and re-layouts  27.7 us (5%)
  between operations  14.1 us (3%)
  other arithmetic  13.7 us (3%)
    while x6, waiting for transfers between devices  197 us
    reduce_scatter x1, waiting for transfers between devices, local(): lax.psum_scatter(jnp.einsum('pn,prc->nrc', match, right_grad, precision=l...  63.2 us
    all_gather x2, waiting for transfers between devices, process(): correlation = jnp.sum(lax.all_gather(correlation_part, 'orb'), axis=0)  54 us
    all_gather x2, blocking collectives, process(): lax.all_gather(left_rows, 'orb', axis=1, tiled=True)  48.1 us
    all_gather x2, blocking collectives, process(): lax.all_gather(moved_rows, 'orb', axis=1, tiled=True)  44.3 us
    all_gather x1, waiting for transfers between devices, local(): everyone = lax.all_gather(orbitals, 'det', axis=0, tiled=True)  39.4 us
    dot_general x2, matrix products, process(): jnp.einsum('bqsc,bqdc->sbd', applied, scaled, preferred_element_type=jnp....  15.3 us
    dot_general x2, matrix products, process(): jnp.einsum('bsc,qst->bqct', left_full, dfit, preferred_element_type=jnp.f...  11.5 us
  transfers between devices with their start and end apart: 6, of which 6 were waited for; matrix products, arithmetic and copies ran while one was open for 4% of the time, Pallas kernels for 0%

profile of v1, /device:TPU:4, one launch (start us, length us, event | category | flops | bytes accessed | tf_op | source)
XLA Modules:
  0.0 545.2 jit_solution(15788098546302673662)
XLA Ops:
  8.6 1.5 gather_fusion
  12.1 39.4 %all-gather.9.cloned.1.call-done = bf16[64,64,256]{2,1,0:T(8,128)(2,1)} async-done(((bf16[4,64,256]{2,1,0:T(8,128)(2,1)}), bf16[64,64,256]{2,1,0:T(8,128)(2,1)}) %all-gather.9.cloned.1.call-update) | async-done | bytes 2097168 | tf_op jit(solution)/shard_map/all_gather | solution.py:63
  51.6 2.1 gather_fusion.1
  53.8 411.1 %while.15 = (s32[]{:T(128)}, f32[2,64,256]{2,0,1:T(2,128)}, f32[2,64,256]{2,0,1:T(2,128)}, f32[2]{0:T(128)S(1)}, s32[2,4]{1,0:T(2,128)}, /*index=5*/bf16[2,64,25...) while((s32[]{:T(128)}, f32[2,64,256]{2,0,1:T(2,128)}, ...), condition=%wide.region_3.4_spmd, body=%wide.region_0.3_spmd.sunk | while | flops 7227981824 | bytes 80483936 | solution.py:84
  53.9 0.9 fusion.130
  56.7 24.2 %all_gather.33 = bf16[1,1024,256]{2,1,0:T(8,128)(2,1)S(1)} all-gather(bf16[1,64,256]{2,1,0:T(8,128)(2,1)S(1)} %constant_dynamic-slice_fusion.6), channel_id=1, replica_groups=mesh['det'=16,'orb'=16] {'orb'}, dimensions={1}, use_global_device_ids=true | all-gather | bytes 557056 | tf_op jit(solution)/shard_map/while/body/eval_jaxpr/all_gather | solution.py:30
  80.9 5.8 %convolution_convert_fusion.4 = bf16[256,4,1024]{2,0,1:T(8,128)(2,1)S(1)} fusion(bf16[4,1024,1024]{2,1,0:T(8,128)(2,1)} %get-tuple-element.282, bf16[1,1024,256]{2,1,0:T(8,128)(2,1)S(1)} %all_gather.33), kind=kOutput, calls=%fused_computation.10.clone.1 | convolution fusion | flops 2148532224 | bytes 11010048 | tf_op jit(solution)/shard_map/while/body/eval_jaxpr/bsc,qst->bqct/dot_general | solution.py:36
  86.7 25.9 %all-gather.11.cloned.1.call-done = f32[4096,256]{1,0:T(8,128)} async-done(((f32[256,256]{1,0:T(8,128)}), f32[4096,256]{1,0:T(8,128)}) %all-gather.11.cloned.1.call-update) | async-done | bytes 4194320 | tf_op jit(solution)/shard_map/while/body/eval_jaxpr/all_gather | solution.py:24
  112.6 2.5 reduce.5
  117.4 22.2 %all-gather.5 = bf16[1024,256]{1,0:T(8,128)(2,1)S(1)} all-gather(bf16[64,256]{1,0:T(8,128)(2,1)S(1)} %convolution_convert_fusion.5), channel_id=3, replica_groups=mesh['det'=16,'orb'=16] {'orb'}, dimensions={0}, use_global_device_ids=true | all-gather | bytes 557056 | tf_op jit(solution)/shard_map/while/body/eval_jaxpr/all_gather | solution.py:31
  142.7 7.6 %fusion.137 = f32[1024,1,256]{0,2,1:T(8,128)} fusion(bf16[4,256,256]{2,1,0:T(8,128)(2,1)} %copy-done, bf16[4,1024,1024]{2,1,0:T(8,128)(2,1)} %get-tuple-element.282, bf16[1024,256]{1,0:T(8,128)(2,1)} %copy-done.1), kind=kOutput, calls=%fused_computation.12.clone.1 | convolution fusion | flops 2685403136 | bytes 10485760 | tf_op jit(solution)/shard_map/while/body/eval_jaxpr/bqsc,bqdc->sbd/dot_general | solution.py:44
  150.3 1.4 pad_maximum_fusion.2
  151.7 2.4 copy.46
  155.9 98.4 %all-reduce.5.cloned.1.call-done = f32[1024,2,256]{2,1,0:T(2,128)} async-done(((f32[1024,2,256]{2,1,0:T(2,128)}), f32[1024,2,256]{2,1,0:T(2,128)}) %all-reduce.5.cloned.1.call-update) | async-done | bytes 2097168 | tf_op jit(solution)/shard_map/while
  254.4 1.1 constant_dynamic-slice_fusion.7
  255.9 0.9 dynamic_update_slice.16
  256.8 0.9 dynamic_update_slice.17
  258.4 0.9 fusion.130
  261.3 23.9 %all_gather.33 = bf16[1,1024,256]{2,1,0:T(8,128)(2,1)S(1)} all-gather(bf16[1,64,256]{2,1,0:T(8,128)(2,1)S(1)} %constant_dynamic-slice_fusion.6), channel_id=1, replica_groups=mesh['det'=16,'orb'=16] {'orb'}, dimensions={1}, use_global_device_ids=true | all-gather | bytes 557056 | tf_op jit(solution)/shard_map/while/body/eval_jaxpr/all_gather | solution.py:30
  285.2 5.8 %convolution_convert_fusion.4 = bf16[256,4,1024]{2,0,1:T(8,128)(2,1)S(1)} fusion(bf16[4,1024,1024]{2,1,0:T(8,128)(2,1)} %get-tuple-element.282, bf16[1,1024,256]{2,1,0:T(8,128)(2,1)S(1)} %all_gather.33), kind=kOutput, calls=%fused_computation.10.clone.1 | convolution fusion | flops 2148532224 | bytes 11010048 | tf_op jit(solution)/shard_map/while/body/eval_jaxpr/bsc,qst->bqct/dot_general | solution.py:36
  290.9 28.1 %all-gather.11.cloned.1.call-done = f32[4096,256]{1,0:T(8,128)} async-done(((f32[256,256]{1,0:T(8,128)}), f32[4096,256]{1,0:T(8,128)}) %all-gather.11.cloned.1.call-update) | async-done | bytes 4194320 | tf_op jit(solution)/shard_map/while/body/eval_jaxpr/all_gather | solution.py:24
  319.0 2.5 reduce.5
  323.9 22.2 %all-gather.5 = bf16[1024,256]{1,0:T(8,128)(2,1)S(1)} all-gather(bf16[64,256]{1,0:T(8,128)(2,1)S(1)} %convolution_convert_fusion.5), channel_id=3, replica_groups=mesh['det'=16,'orb'=16] {'orb'}, dimensions={0}, use_global_device_ids=true | all-gather | bytes 557056 | tf_op jit(solution)/shard_map/while/body/eval_jaxpr/all_gather | solution.py:31
  349.1 7.6 %fusion.137 = f32[1024,1,256]{0,2,1:T(8,128)} fusion(bf16[4,256,256]{2,1,0:T(8,128)(2,1)} %copy-done, bf16[4,1024,1024]{2,1,0:T(8,128)(2,1)} %get-tuple-element.282, bf16[1024,256]{1,0:T(8,128)(2,1)} %copy-done.1), kind=kOutput, calls=%fused_computation.12.clone.1 | convolution fusion | flops 2685403136 | bytes 10485760 | tf_op jit(solution)/shard_map/while/body/eval_jaxpr/bqsc,bqdc->sbd/dot_general | solution.py:44
  356.8 1.4 pad_maximum_fusion.2
  358.2 2.4 copy.46
  362.4 98.4 %all-reduce.5.cloned.1.call-done = f32[1024,2,256]{2,1,0:T(2,128)} async-done(((f32[1024,2,256]{2,1,0:T(2,128)}), f32[1024,2,256]{2,1,0:T(2,128)}) %all-reduce.5.cloned.1.call-update) | async-done | bytes 2097168 | tf_op jit(solution)/shard_map/while
  460.8 1.1 constant_dynamic-slice_fusion.7
  464.9 2.8 fusion.39
  467.7 4.4 copy.30
  473.5 63.2 %reduce-scatter.2.cloned.1.call-done = f32[4,64,256]{2,1,0:T(8,128)} async-done(((f32[64,64,256]{2,1,0:T(8,128)}), f32[4,64,256]{2,1,0:T(8,128)}) %reduce-scatter.2.cloned.1.call-update) | async-done | bytes 262160 | tf_op jit(solution)/shard_map/reduce_scatter | solution.py:91
  536.7 1.7 copy_add_fusion
  (88 shorter events, 24.9 us)
Async XLA Ops:
  6.5 45.0 %all-gather.9.cloned.1.call-start = ((), (), s32[]{:S(2)}) async-start(), calls=%async_computation.1 | async-start | bytes 2228224 | tf_op jit(solution)/shard_map/all_gather | solution.py:63
  53.8 411.1 %copy-start.7 = (s32[2]{0:T(128)S(1)}, s32[2]{0:T(128)}, u32[]{:S(2)}) copy-start(s32[2]{0:T(128)} %param.12) | copy-start | bytes 28
  53.8 58.8 %all-gather.11.cloned.1.call-start = ((), (), s32[]{:S(2)}) async-start(), calls=%async_computation.3 | async-start | bytes 4456448 | tf_op jit(solution)/shard_map/while/body/eval_jaxpr/all_gather | solution.py:24
  54.8 199.6 %all-reduce.5.cloned.1.call-start = ((), (), s32[]{:S(2)}) async-start(), calls=%async_computation.4 | async-start | bytes 4194304 | tf_op jit(solution)/shard_map/while
  139.6 0.8 copy-start.1
  141.1 0.8 copy-start
  154.1 0.7 copy-start.8
  154.1 101.8 %copy-start.4 = (f32[2,64,256]{2,0,1:T(2,128)S(1)}, f32[2,64,256]{2,0,1:T(2,128)}, u32[]{:S(2)}) copy-start(f32[2,64,256]{2,0,1:T(2,128)} %get-tuple-element.261) | copy-start | bytes 393220 | tf_op jit(solution)/shard_map/while
  154.1 102.7 %copy-start.2 = (f32[2,64,256]{2,0,1:T(2,128)S(1)}, f32[2,64,256]{2,0,1:T(2,128)}, u32[]{:S(2)}) copy-start(f32[2,64,256]{2,0,1:T(2,128)} %get-tuple-element.262) | copy-start | bytes 393220 | tf_op jit(solution)/shard_map/while
  256.8 1.0 copy-start.5
  257.8 0.7 copy-start.3
  258.4 60.6 %all-gather.11.cloned.1.call-start = ((), (), s32[]{:S(2)}) async-start(), calls=%async_computation.3 | async-start | bytes 4456448 | tf_op jit(solution)/shard_map/while/body/eval_jaxpr/all_gather | solution.py:24
  259.4 201.5 %all-reduce.5.cloned.1.call-start = ((), (), s32[]{:S(2)}) async-start(), calls=%async_computation.4 | async-start | bytes 4194304 | tf_op jit(solution)/shard_map/while
  346.0 0.8 copy-start.1
  347.6 0.8 copy-start
  360.6 0.7 copy-start.8
  360.6 101.8 %copy-start.4 = (f32[2,64,256]{2,0,1:T(2,128)S(1)}, f32[2,64,256]{2,0,1:T(2,128)}, u32[]{:S(2)}) copy-start(f32[2,64,256]{2,0,1:T(2,128)} %get-tuple-element.261) | copy-start | bytes 393220 | tf_op jit(solution)/shard_map/while
  360.6 102.7 %copy-start.2 = (f32[2,64,256]{2,0,1:T(2,128)S(1)}, f32[2,64,256]{2,0,1:T(2,128)}, u32[]{:S(2)}) copy-start(f32[2,64,256]{2,0,1:T(2,128)} %get-tuple-element.262) | copy-start | bytes 393220 | tf_op jit(solution)/shard_map/while
  463.3 1.0 copy-start.5
  464.2 0.7 copy-start.3
  464.9 71.8 %reduce-scatter.2.cloned.1.call-start = ((), (), s32[]{:S(2)}) async-start(), calls=%async_computation.2 | async-start | bytes 4456448 | tf_op jit(solution)/shard_map/reduce_scatter | solution.py:91
  472.1 0.9 copy-start.6
Sparse Core Ops, SparseCore 0:
  9.2 42.3 all-gather.8
  57.1 55.4 all-gather.10
  154.2 100.0 all-reduce.4
  261.3 57.6 all-gather.10
  360.7 100.0 all-reduce.4
  472.2 64.3 reduce-scatter.1
